TPU v7x, 32 devices: a whole 2x2x4 slice. The times are simulated.
32 devices in a mesh: row: 2 (over core), col: 2 (over x), seq: 8 (over z, y).
Axes of the slice: x: 2, y: 2, z: 4, core: 2. Of those that a mesh axis runs over, the one named last changes fastest.
Arguments:
- states: bfloat16 [128, 4, 5120], P('col', None, 'row'), may hold values from -64 to 64
- norm_gain: float32 [5120], P('row'), may hold values from 0.1 to 1.9
- wq: bfloat16 [5120, 4096], P('row', 'col'), may hold values from -0.078125 to 0.078125
- wk: bfloat16 [5120, 1024], P('row', 'col'), may hold values from -0.21875 to 0.21875
- wv: bfloat16 [5120, 1024], P('row', 'col'), may hold values from -0.078125 to 0.078125
- wo: bfloat16 [4096, 5120], P('col', 'row'), may hold values from -0.09375 to 0.09375
- lengths: int32 [128], P('row'), may hold values from 1 to 8192, as said below
- slot_request: int32 [800], P(('row', 'seq')), may hold values from 0 to 64, as said below
- slot_block_number: int32 [800], P(('row', 'seq')), may hold values from 0 to 63, as said below
- paged_key_cache: bfloat16 [800, 128, 1024], P(('row', 'seq'), None, 'col'), may hold values from -120 to 120
- paged_value_cache: bfloat16 [800, 128, 1024], P(('row', 'seq'), None, 'col'), may hold values from -6 to 6
Outputs:
- attended: bfloat16 [128, 4, 5120], P('col', None, 'row')
- new_keys: bfloat16 [128, 4, 1024], P('row', None, 'col')
- new_values: bfloat16 [128, 4, 1024], P('row', None, 'col')
Inputs may be any that keep to these rules, and one draw needn't show every extreme that they name: `lengths`: within every 64 consecutive requests, 8 have exactly 8192 cached tokens and the others fewer than 128. `slot_request`: each request's block 0 and every block that holds a position visible to one of its steps stand in exactly one slot of its index of row; a long request has exactly 33 slots. 64 marks an empty slot; every index of row has empty slots. `slot_block_number`: 0 in empty slots.
All inputs are finite; a program needn't handle non-finite values.
Results may differ from a plain program's by a relative error of at most 0.034.
Values may be sent and summed in bfloat16 or wider, within the bound.
No kernel may reach another device: no remote copies, remote signals or barrier semaphores. Data moves between devices by JAX's collectives and lax.ppermute only.
A program may use at most 192 MiB of HBM per device.

v0:
```python
import math
import jax
import jax.numpy as jnp
from jax import lax
from jax.sharding import PartitionSpec as P

D = 5120
HEAD_SIZE = 128
WINDOW = 4096
SINK = 4
QUERY_PER_KEY = 4
EPSILON = 1e-05
NEGATIVE_FILL = -1e30
ROPE_BASE = 100000000.0


def rotary_apply(values, token_positions):
    half_dim = values.shape[-1] // 2
    frequency = ROPE_BASE ** (-(jnp.arange(half_dim, dtype=jnp.float32) * 2.0 / values.shape[-1]))
    angles = (token_positions.astype(jnp.float32)[..., None] * frequency)[..., None, :]
    cosine = jnp.cos(angles)
    sine_part = jnp.sin(angles)
    lower = values[..., :half_dim]
    upper = values[..., half_dim:]
    return jnp.concatenate(
        [lower * cosine - upper * sine_part, upper * cosine + lower * sine_part], -1
    )


def slot_parts(query_rows, lengths, slot_request, slot_block_number, key_rows, value_rows):
    req_count = query_rows.shape[0]
    step_count = query_rows.shape[1]
    block_len = key_rows.shape[1]
    picked = jnp.minimum(slot_request, req_count - 1)
    in_use = slot_request < req_count
    slot_queries = query_rows[picked]
    scores = jnp.einsum(
        "nsagh,nbah->nasgb", slot_queries, key_rows, preferred_element_type=jnp.float32
    ) * (1.0 / math.sqrt(HEAD_SIZE))
    key_pos = (
        slot_block_number[:, None] * block_len + jnp.arange(block_len, dtype=jnp.int32)[None, :]
    )
    own_len = lengths[picked]
    query_pos = own_len[:, None] + jnp.arange(step_count, dtype=jnp.int32)[None, :]
    visible = (
        in_use[:, None, None]
        & (key_pos[:, None, :] < own_len[:, None, None])
        & ((key_pos[:, None, :] < SINK) | (key_pos[:, None, :] > query_pos[:, :, None] - WINDOW))
    )
    visible = visible[:, None, :, None, :]
    slot_peak = jnp.max(jnp.where(visible, scores, NEGATIVE_FILL), -1)
    weights = jnp.where(visible, jnp.exp(scores - slot_peak[..., None]), 0.0)
    slot_total = jnp.sum(weights, -1)
    slot_acc = jnp.einsum(
        "nasgb,nbah->nasgh",
        weights.astype(jnp.bfloat16),
        value_rows,
        preferred_element_type=jnp.float32,
    )
    member = slot_request[None, :] == jnp.arange(req_count, dtype=jnp.int32)[:, None]
    local_peak = jnp.max(
        jnp.where(member[:, :, None, None, None], slot_peak[None], NEGATIVE_FILL), 1
    )
    return (local_peak, (slot_peak, slot_total, slot_acc, member, picked))


def pool_sums(held, running_peak):
    slot_peak, slot_total, slot_acc, member, picked = held
    factor = jnp.exp(slot_peak - running_peak[picked])
    as_member = member.astype(jnp.float32)
    running_totals = jnp.einsum(
        "rn,nasg->rasg", as_member, slot_total * factor, precision=lax.Precision.HIGHEST
    )
    weighted_values = jnp.einsum(
        "rn,nasgh->rasgh", as_member, slot_acc * factor[..., None], precision=lax.Precision.HIGHEST
    )
    return (running_totals, weighted_values)


def fresh_part(query_rows, key_all, value_all):
    step_count = query_rows.shape[1]
    used = key_all.shape[1]
    scores = jnp.einsum(
        "rsagh,ruah->rasgu", query_rows, key_all, preferred_element_type=jnp.float32
    ) * (1.0 / math.sqrt(HEAD_SIZE))
    causal = (
        jnp.arange(used, dtype=jnp.int32)[None, :]
        <= jnp.arange(step_count, dtype=jnp.int32)[:, None]
    )
    causal = causal[None, None, :, None, :]
    running_peak = jnp.max(jnp.where(causal, scores, NEGATIVE_FILL), -1)
    weights = jnp.where(causal, jnp.exp(scores - running_peak[..., None]), 0.0)
    running_totals = jnp.sum(weights, -1)
    weighted_values = jnp.einsum(
        "rasgu,ruah->rasgh",
        weights.astype(jnp.bfloat16),
        value_all,
        preferred_element_type=jnp.float32,
    )
    return (running_peak, running_totals, weighted_values)


def merge_parts(earlier, later):
    running_peak = jnp.maximum(earlier[0], later[0])
    first_factor = jnp.exp(earlier[0] - running_peak)
    second_factor = jnp.exp(later[0] - running_peak)
    running_totals = earlier[1] * first_factor + later[1] * second_factor
    weighted_values = earlier[2] * first_factor[..., None] + later[2] * second_factor[..., None]
    return (running_peak, running_totals, weighted_values)


def on_device(
    states,
    norm_gain,
    wq,
    wk,
    wv,
    wo,
    lengths,
    slot_request,
    slot_block_number,
    paged_key_cache,
    paged_value_cache,
):
    q_width = wq.shape[1]
    k_width = wk.shape[1]
    heads_kv = k_width // HEAD_SIZE
    req_count = lengths.shape[0]
    block_len = paged_key_cache.shape[1]
    key_rows = paged_key_cache.reshape(paged_key_cache.shape[0], block_len, heads_kv, HEAD_SIZE)
    value_rows = paged_value_cache.reshape(
        paged_value_cache.shape[0], block_len, heads_kv, HEAD_SIZE
    )
    step_count = states.shape[1]
    as_float = states.astype(jnp.float32)
    squares = lax.psum(jnp.sum(as_float * as_float, -1), "row")
    normed = (as_float * lax.rsqrt(squares / D + EPSILON)[..., None] * norm_gain).astype(
        jnp.bfloat16
    )
    gathered = lax.all_gather(normed, "col", axis=0, tiled=True)
    piece_rows = gathered.reshape(req_count * lax.axis_size("row") * step_count, -1)
    parts_out = [
        jnp.dot(piece_rows, matrix, preferred_element_type=jnp.float32) for matrix in (wq, wk, wv)
    ]
    output_projected = lax.psum_scatter(
        jnp.concatenate(parts_out, axis=-1)
        .reshape(req_count * lax.axis_size("row"), step_count, -1)
        .astype(jnp.bfloat16),
        "row",
        scatter_dimension=0,
        tiled=True,
    ).astype(jnp.float32)
    token_positions = lengths[:, None] + jnp.arange(step_count, dtype=jnp.int32)[None, :]
    query_rows = rotary_apply(
        output_projected[..., :q_width].reshape(req_count, step_count, -1, HEAD_SIZE),
        token_positions,
    ).astype(jnp.bfloat16)
    query_rows = query_rows.reshape(req_count, step_count, heads_kv, QUERY_PER_KEY, HEAD_SIZE)
    current_key = rotary_apply(
        output_projected[..., q_width : q_width + k_width].reshape(
            req_count, step_count, heads_kv, HEAD_SIZE
        ),
        token_positions,
    ).astype(jnp.bfloat16)
    current_value = (
        output_projected[..., q_width + k_width :]
        .reshape(req_count, step_count, heads_kv, HEAD_SIZE)
        .astype(jnp.bfloat16)
    )
    local_peak, held = slot_parts(
        query_rows, lengths, slot_request, slot_block_number, key_rows, value_rows
    )
    running_peak = lax.pmax(local_peak, "seq")
    running_totals, weighted_values = pool_sums(held, running_peak)
    running_totals, weighted_values = (
        lax.psum(running_totals.astype(jnp.bfloat16), "seq").astype(jnp.float32),
        lax.psum(weighted_values.astype(jnp.bfloat16), "seq").astype(jnp.float32),
    )
    fresh = fresh_part(query_rows, current_key, current_value)
    running_peak, running_totals, weighted_values = merge_parts(
        (running_peak, running_totals, weighted_values), fresh
    )
    heads_out = (
        (weighted_values / running_totals[..., None])
        .transpose(0, 2, 1, 3, 4)
        .reshape(req_count, step_count, -1)
        .astype(jnp.bfloat16)
    )
    piece_rows = lax.all_gather(heads_out, "row", axis=0, tiled=True)
    row_count = piece_rows.shape[0]
    product = jnp.dot(
        piece_rows.reshape(row_count * step_count, -1), wo, preferred_element_type=jnp.float32
    )
    partials = product.reshape(row_count, step_count, -1)
    attended = lax.psum_scatter(
        partials.astype(jnp.bfloat16), "col", scatter_dimension=0, tiled=True
    )
    return (
        attended,
        current_key.reshape(req_count, step_count, k_width),
        current_value.reshape(req_count, step_count, k_width),
    )


def solution(mesh):
    in_specs = (
        P("col", None, "row"),
        P("row"),
        P("row", "col"),
        P("row", "col"),
        P("row", "col"),
        P("col", "row"),
        P("row"),
        P(("row", "seq")),
        P(("row", "seq")),
        P(("row", "seq"), None, "col"),
        P(("row", "seq"), None, "col"),
    )
    out_specs = (P("col", None, "row"), P("row", None, "col"), P("row", None, "col"))
    return jax.shard_map(
        on_device, mesh=mesh, in_specs=in_specs, out_specs=out_specs, check_vma=False
    )
```

profile of v0, /device:TPU:0, one launch (start us, length us, event | category | flops | bytes accessed | tf_op | source)
XLA Modules:
  0.0 341.6 jit_solution(11022406717256435798)
XLA Ops:
  7.2 2.2 fusion.9
  9.5 2.6 psum.21
  12.2 3.1 fusion.11
  15.4 41.7 %all-gather.3.cloned.1.call-done = bf16[128,4,2560]{2,1,0:T(4,128)(2,1)} async-done(((bf16[64,4,2560]{2,1,0:T(4,128)(2,1)}), bf16[128,4,2560]{2,1,0:T(4,128)(2,1)}) %all-gather.3.cloned.1.call-update) | async-done | bytes 2621456 | tf_op jit(solution)/shard_map/all_gather | solution.py:140
  57.1 5.3 %reshape.218 = bf16[512,2560]{1,0:T(8,128)(2,1)} reshape(bf16[128,4,2560]{2,1,0:T(4,128)(2,1)} %all-gather.3.cloned.1.call-done) | data formatting | bytes 5242880 | tf_op jit(solution)/shard_map/reshape | solution.py:141
  62.5 3.4 convolution_convert_fusion.1
  67.4 8.5 %convolution_convert_fusion = bf16[512,2048]{1,0:T(8,128)(2,1)S(1)} fusion(bf16[512,2560]{1,0:T(8,128)(2,1)S(1)} %copy-done.4, bf16[2560,2048]{1,0:T(8,128)(2,1)} %param.13), kind=kOutput, calls=%fused_computation.13 | convolution fusion | flops 5369757696 | bytes 15204352 | tf_op jit(solution)/shard_map/dot_general | solution.py:143
  76.2 2.7 convert_element_type.70
  81.8 12.3 %reshape.220 = bf16[50,128,4,128]{3,2,1,0:T(4,128)(2,1)} reshape(bf16[50,128,512]{2,1,0:T(8,128)(2,1)} %param.20) | data formatting | bytes 13107200 | tf_op jit(solution)/shard_map/reshape | solution.py:130
  94.1 12.4 %reshape.221 = bf16[50,128,4,128]{3,2,1,0:T(4,128)(2,1)} reshape(bf16[50,128,512]{2,1,0:T(8,128)(2,1)} %param.21) | data formatting | bytes 13107200 | tf_op jit(solution)/shard_map/reshape | solution.py:131
  114.8 2.4 reshape.258
  122.8 10.3 %fusion.33 = f32[64,4,4,4,4]{3,4,2,1,0:T(4,128)S(1)} fusion(bf16[64,4,4,4,128]{4,3,2,0,1:T(4,128)(2,1)S(1)} %pad_maximum_fusion.1, bf16[64,4,4,64]{3,1,2,0:T(4,128)(2,1)} %get-tuple-element.34, bf16[64,4,4,64]{3,1,2,0:T(4,128)(2,1)S(1)} %get-tuple-element.33), kind=kOutput, calls=%fused_computation.49 | convolution fusion | flops 4718592 | bytes 1376256 | tf_op jit(solution)/shard_map/rsagh,ruah->rasgu/dot_general | solution.py:83
  134.8 6.8 %select_reduce_fusion.1 = (f32[50,4,4,4]{3,2,1,0:T(4,128)S(1)}, f32[50,4,4,4,128]{4,3,2,1,0:T(4,128)S(1)}) fusion(pred[50,4,128]{2,1,0:T(4,128)(4,1)S(1)} %or_and_fusion, bf16[50,4,4,4,128]{4,3,1,2,0:T(4,128)(2,1)} %gather_fusion.1, bf16[50,128,4,128,1]{3,2,1,0,4:T(4,128)(2,1)} %bitcast.60), kind=kOutput, calls=%fused_computation.27 | convolution fusion | flops 106083200 | bytes 9049600 | tf_op jit(solution)/shard_map/nsagh,nbah->nasgb/dot_general | solution.py:37
  142.7 37.1 %pmax.7 = f32[64,4,4,4]{0,3,2,1:T(4,128)S(1)} all-reduce(f32[64,4,4,4]{0,3,2,1:T(4,128)S(1)} %select_reduce_fusion), channel_id=1, replica_groups=mesh['row'=2,'col'=2,'seq'=8] {'seq'}, use_global_device_ids=true, to_apply=%region_5.6 | all-reduce | flops 4096 | bytes 32768 | tf_op jit(solution)/shard_map/pmax | solution.py:173
  179.8 2.7 fusion.24
  183.9 4.5 %fusion.20 = f32[50,4,4,4,128]{4,3,2,1,0:T(4,128)S(1)} fusion(bf16[50,128,4,128,1]{3,2,1,0,4:T(4,128)(2,1)} %bitcast.59, f32[50,4,4,4,128]{4,3,2,1,0:T(4,128)S(1)} %get-tuple-element.42, f32[50,4,4,4]{3,2,1,0:T(4,128)S(1)} %bitcast.67, f32[50,4,4,4]{3,2,1,0:T(4,128)S(1)} %get-tuple-element.41, pred[50,4,128]{2,1,0:T(4,128)(4,1)} %copy-done.9), kind=kOutput, calls=%fused_computation.30 | convolution fusion | flops 106905600 | bytes 9881600 | tf_op jit(solution)/shard_map/nasgb,nbah->nasgh/dot_general | solution.py:54
  188.5 3.2 fusion.17
  196.5 33.6 %psum.23 = bf16[64,4,4,4]{0,3,2,1:T(4,128)(2,1)S(1)} all-reduce(bf16[64,4,4,4]{0,3,2,1:T(4,128)(2,1)S(1)} %convert_element_type.80), channel_id=1, replica_groups=mesh['row'=2,'col'=2,'seq'=8] {'seq'}, use_global_device_ids=true, to_apply=%region_9.10 | all-reduce | flops 4096 | bytes 16384 | tf_op jit(solution)/shard_map/psum | solution.py:176
  230.7 35.7 %all-reduce.4.cloned.1.call-done = bf16[64,4,4,4,128]{4,0,3,2,1:T(8,128)(2,1)} async-done(((bf16[64,4,4,4,128]{4,0,3,2,1:T(8,128)(2,1)}), bf16[64,4,4,4,128]{4,0,3,2,1:T(8,128)(2,1)}) %all-reduce.4.cloned.1.call-update) | async-done | bytes 1048592 | tf_op jit(solution)/shard_map/psum | solution.py:177
  266.3 3.4 fusion.23
  272.2 10.3 %all-gather.5.cloned.1.call-done = bf16[128,4,2048]{2,0,1:T(8,128)(2,1)} async-done(((bf16[64,4,2048]{2,0,1:T(8,128)(2,1)}), bf16[128,4,2048]{2,0,1:T(8,128)(2,1)}) %all-gather.5.cloned.1.call-update) | async-done | bytes 2097168 | tf_op jit(solution)/shard_map/all_gather | solution.py:189
  282.5 10.0 %fusion.6 = bf16[128,4,2560]{2,0,1:T(8,128)(2,1)} fusion(bf16[128,4,2048]{2,0,1:T(8,128)(2,1)} %all-gather.5.cloned.1.call-done, bf16[2048,2560]{1,0:T(8,128)(2,1)} %param.16), kind=kOutput, calls=%fused_computation.9 | convolution fusion | flops 5370019840 | bytes 15204352 | tf_op jit(solution)/shard_map/dot_general | solution.py:191
  294.6 36.9 %reduce-scatter.2.cloned.1.call-done = bf16[64,4,2560]{2,0,1:T(8,128)(2,1)} async-done(((bf16[128,4,2560]{2,0,1:T(8,128)(2,1)}), bf16[64,4,2560]{2,0,1:T(8,128)(2,1)}) %reduce-scatter.2.cloned.1.call-update) | async-done | bytes 1310736 | tf_op jit(solution)/shard_map/reduce_scatter | solution.py:195
  331.5 3.4 copy.155
  (95 shorter events, 32.1 us)
Async XLA Ops:
  7.2 55.3 %copy-start = (bf16[2560,512]{1,0:T(8,128)(2,1)S(1)}, bf16[2560,512]{1,0:T(8,128)(2,1)}, u32[]{:S(2)}) copy-start(bf16[2560,512]{1,0:T(8,128)(2,1)} %param.15) | copy-start | bytes 7864324
  7.2 50.0 %all-gather.3.cloned.1.call-start = ((), (), s32[]{:S(2)}) async-start(), calls=%async_computation.1 | async-start | bytes 3932160 | tf_op jit(solution)/shard_map/all_gather | solution.py:140
  15.4 94.1 %all-reduce.6.cloned.1.call-start = ((), (), s32[]{:S(2)}) async-start(), calls=%async_computation.5 | async-start | bytes 6291456
  62.5 3.4 %copy-start.4 = (bf16[512,2560]{1,0:T(8,128)(2,1)S(1)}, bf16[512,2560]{1,0:T(8,128)(2,1)}, u32[]{:S(2)}) copy-start(bf16[512,2560]{1,0:T(8,128)(2,1)} %reshape.218) | copy-start | bytes 7864324
  62.5 3.4 %copy-start.15 = (bf16[2560,512]{1,0:T(8,128)(2,1)S(1)}, bf16[2560,512]{1,0:T(8,128)(2,1)}, u32[]{:S(2)}) copy-start(bf16[2560,512]{1,0:T(8,128)(2,1)} %param.14) | copy-start | bytes 7864324
  78.9 0.7 copy-start.12
  78.9 0.7 copy-start.2
  78.9 187.4 %all-reduce.4.cloned.1.call-start = ((), (), s32[]{:S(2)}) async-start(), calls=%async_computation.2 | async-start | bytes 2097152 | tf_op jit(solution)/shard_map/psum | solution.py:177
  79.6 41.0 %copy-start.11 = (s32[1024]{0:T(1024)}, s32[1024]{0:T(1024)S(1)}, u32[]{:S(2)}) copy-start(s32[1024]{0:T(1024)S(1)} %pad_clamp_fusion) | copy-start | bytes 12292
  94.1 12.4 %copy-start.17 = (u32[32]{0:T(128)S(1)}, u32[32]{0:T(128)}, u32[]{:S(2)}) copy-start(u32[32]{0:T(128)} %constant.40) | copy-start | bytes 388
  94.1 14.2 %copy-start.16 = (s32[50]{0:T(128)S(1)}, s32[50]{0:T(128)}, u32[]{:S(2)}) copy-start(s32[50]{0:T(128)} %param.19) | copy-start | bytes 604
  109.4 25.4 %copy-start.9 = (pred[50,4,128]{2,1,0:T(4,128)(4,1)}, pred[50,4,128]{2,1,0:T(4,128)(4,1)S(1)}, u32[]{:S(2)}) copy-start(pred[50,4,128]{2,1,0:T(4,128)(4,1)S(1)} %or_and_fusion) | copy-start | bytes 76804
  111.3 2.3 copy-start.3
  114.8 8.0 %copy-start.5 = (bf16[64,4,4,64]{3,1,2,0:T(4,128)(2,1)}, bf16[64,4,4,64]{3,1,2,0:T(4,128)(2,1)S(1)}, u32[]{:S(2)}) copy-start(bf16[64,4,4,64]{3,1,2,0:T(4,128)(2,1)S(1)} %get-tuple-element.33) | copy-start | bytes 393220
  134.8 6.9 %copy-start.10 = (pred[64,50]{0,1:T(8,128)(4,1)S(1)}, pred[64,50]{0,1:T(8,128)(4,1)}, u32[]{:S(2)}) copy-start(pred[64,50]{0,1:T(8,128)(4,1)} %iota_compare_fusion) | copy-start | bytes 9604
  183.9 4.6 %copy-start.13 = (s32[50]{0:T(128)S(1)}, s32[50]{0:T(128)}, u32[]{:S(2)}) copy-start(s32[50]{0:T(128)} %param.18) | copy-start | bytes 604
  188.5 3.3 copy-start.14
  191.7 90.8 %all-gather.5.cloned.1.call-start = ((), (), s32[]{:S(2)}) async-start(), calls=%async_computation.3 | async-start | bytes 3145728 | tf_op jit(solution)/shard_map/all_gather | solution.py:189
  194.0 36.1 %copy-start.8 = (bf16[64,4,512]{2,1,0:T(4,128)(2,1)S(1)}, bf16[64,4,512]{2,1,0:T(4,128)(2,1)}, u32[]{:S(2)}) copy-start(bf16[64,4,512]{2,1,0:T(4,128)(2,1)} %slice.47) | copy-start | bytes 786436
  272.2 59.3 %reduce-scatter.2.cloned.1.call-start = ((), (), s32[]{:S(2)}) async-start(), calls=%async_computation.4 | async-start | bytes 3932160 | tf_op jit(solution)/shard_map/reduce_scatter | solution.py:195
  292.6 0.9 copy-start.6
  292.6 1.0 copy-start.7
  293.6 41.3 %copy-start.1 = (bf16[2560,512]{1,0:T(8,128)(2,1)S(1)}, bf16[2560,512]{1,0:T(8,128)(2,1)}, u32[]{:S(2)}) copy-start(bf16[2560,512]{1,0:T(8,128)(2,1)} %param.15) | copy-start | bytes 7864324
Sparse Core Ops, SparseCore 0:
  15.5 41.5 all-gather.2
  79.0 23.2 all-reduce.5
  191.8 74.4 all-reduce.3
  272.3 10.1 all-gather.4
  292.7 38.7 reduce-scatter.1
where the time goes:
time: 348 us; the launch traced here: 342 us
  waiting for transfers between devices  125 us (36%)
  blocking collectives  73.2 us (21%)
  local copies, waits for them, and re-layouts  57 us (16%)
  matrix products  49.1 us (14%)
  other arithmetic  22.5 us (6%)
  between operations  15 us (4%)
    all_gather x1, waiting for transfers between devices, on_device(): gathered = lax.all_gather(normed, 'col', axis=0, tiled=True)  41.7 us
    pmax x1, blocking collectives, on_device(): running_peak = lax.pmax(local_peak, 'seq')  37.1 us
    reduce_scatter x1, waiting for transfers between devices, on_device(): lax.psum_scatter(partials.astype(jnp.bfloat16), 'col', scatter_dimension=...  36.9 us
    psum x1, waiting for transfers between devices, on_device(): lax.psum(weighted_values.astype(jnp.bfloat16), 'seq').astype(jnp.float32)  35.7 us
    psum x1, blocking collectives, on_device(): lax.psum(running_totals.astype(jnp.bfloat16), 'seq').astype(jnp.float32)  33.6 us
    dot_general x3, matrix products, on_device(): jnp.dot(piece_rows, matrix, preferred_element_type=jnp.float32)  13.4 us
    reshape x1, local copies, waits for them, and re-layouts, on_device(): paged_value_cache.reshape(paged_value_cache.shape[0], block_len, heads_kv...  12.4 us
    reshape x1, local copies, waits for them, and re-layouts, on_device(): paged_key_cache.reshape(paged_key_cache.shape[0], block_len, heads_kv, HE...  12.3 us
  transfers between devices with their start and end apart: 5, of which 4 were waited for; matrix products, arithmetic and copies ran while one was open for 10% of the time, Pallas kernels for 0%

commit v1 on v0

--- a/solution.py
+++ b/solution.py
@@ -172,9 +172,12 @@
     )
     running_peak = lax.pmax(local_peak, "seq")
     running_totals, weighted_values = pool_sums(held, running_peak)
+    run_tell = lambda content, mesh_name: jnp.sum(
+        jax.lax.all_gather(content, axis_name=mesh_name), 0
+    )
     running_totals, weighted_values = (
         lax.psum(running_totals.astype(jnp.bfloat16), "seq").astype(jnp.float32),
-        lax.psum(weighted_values.astype(jnp.bfloat16), "seq").astype(jnp.float32),
+        run_tell(weighted_values.astype(jnp.bfloat16), "seq").astype(jnp.float32),
     )
     fresh = fresh_part(query_rows, current_key, current_value)
     running_peak, running_totals, weighted_values = merge_parts(

time: 348 us -> 398 us (1.14)
  waiting for transfers between devices: 125 us -> 156 us
  blocking collectives: 73.2 us -> 85.6 us
    all_gather x0 -> x1, waiting for transfers between devices: none -> 68.4 us  [on_device(): jax.lax.all_gather(content, axis_name=mesh_name)]
    psum x1 -> x0, waiting for transfers between devices: 35.7 us -> none  [on_device(): lax.psum(weighted_values.astype(jnp.bfloat16), 'seq').astype(jnp.float32)]
    pmax x1, blocking collectives: 37.1 us -> 49.1 us  [on_device(): running_peak = lax.pmax(local_peak, 'seq')]
    reduce_sum x0 -> x2, other arithmetic: none -> 5.84 us  [the longest x1 5.65 us: on_device(): jnp.sum(jax.lax.all_gather(content, axis_name=mesh_name), 0)]
    unnamed x38 -> x52, local copies, waits for them, and re-layouts: 6.14 us -> 8.33 us
  transfers between devices with their start and end apart: 5 -> 5, of which waited for: 4 -> 4; matrix products, arithmetic and copies ran while one was open for 10% -> 12% of each run, Pallas kernels for 0% -> 0%
where the time goes in v1:
time: 398 us; the launch traced here: 392 us
  waiting for transfers between devices  156 us (39%)
  blocking collectives  85.6 us (22%)
  local copies, waits for them, and re-layouts  59.4 us (15%)
  matrix products  49.3 us (12%)
  other arithmetic  26.1 us (7%)
  between operations  15.1 us (4%)
    all_gather x1, waiting for transfers between devices, on_device(): jax.lax.all_gather(content, axis_name=mesh_name)  68.4 us
    pmax x1, blocking collectives, on_device(): running_peak = lax.pmax(local_peak, 'seq')  49.1 us
    all_gather x1, waiting for transfers between devices, on_device(): gathered = lax.all_gather(normed, 'col', axis=0, tiled=True)  41.7 us
    reduce_scatter x1, waiting for transfers between devices, on_device(): lax.psum_scatter(partials.astype(jnp.bfloat16), 'col', scatter_dimension=...  36.8 us
    psum x1, blocking collectives, on_device(): lax.psum(running_totals.astype(jnp.bfloat16), 'seq').astype(jnp.float32)  33.9 us
    dot_general x3, matrix products, on_device(): jnp.dot(piece_rows, matrix, preferred_element_type=jnp.float32)  13.4 us
    reshape x1, local copies, waits for them, and re-layouts, on_device(): paged_value_cache.reshape(paged_value_cache.shape[0], block_len, heads_kv...  12.4 us
    reshape x1, local copies, waits for them, and re-layouts, on_device(): paged_key_cache.reshape(paged_key_cache.shape[0], block_len, heads_kv, HE...  12.3 us
  transfers between devices with their start and end apart: 5, of which 4 were waited for; matrix products, arithmetic and copies ran while one was open for 12% of the time, Pallas kernels for 0%

profile of v1, /device:TPU:0, one launch (start us, length us, event | category | flops | bytes accessed | tf_op | source)
XLA Modules:
  0.0 392.0 jit_solution(11985815563443540572)
XLA Ops:
  7.2 2.2 fusion.9
  9.5 2.6 psum.14
  12.2 3.1 fusion.11
  15.4 41.7 %all-gather.5.cloned.1.call-done = bf16[128,4,2560]{2,1,0:T(4,128)(2,1)} async-done(((bf16[64,4,2560]{2,1,0:T(4,128)(2,1)}), bf16[128,4,2560]{2,1,0:T(4,128)(2,1)}) %all-gather.5.cloned.1.call-update) | async-done | bytes 2621456 | tf_op jit(solution)/shard_map/all_gather | solution.py:140
  57.1 5.3 %reshape.218 = bf16[512,2560]{1,0:T(8,128)(2,1)} reshape(bf16[128,4,2560]{2,1,0:T(4,128)(2,1)} %all-gather.5.cloned.1.call-done) | data formatting | bytes 5242880 | tf_op jit(solution)/shard_map/reshape | solution.py:141
  62.5 3.4 convolution_convert_fusion.1
  67.4 8.5 %convolution_convert_fusion = bf16[512,2048]{1,0:T(8,128)(2,1)S(1)} fusion(bf16[512,2560]{1,0:T(8,128)(2,1)S(1)} %copy-done.4, bf16[2560,2048]{1,0:T(8,128)(2,1)} %param.13), kind=kOutput, calls=%fused_computation.13 | convolution fusion | flops 5369757696 | bytes 15204352 | tf_op jit(solution)/shard_map/dot_general | solution.py:143
  76.2 2.7 convert_element_type.73
  82.3 12.3 %reshape.220 = bf16[50,128,4,128]{3,2,1,0:T(4,128)(2,1)} reshape(bf16[50,128,512]{2,1,0:T(8,128)(2,1)} %param.20) | data formatting | bytes 13107200 | tf_op jit(solution)/shard_map/reshape | solution.py:130
  94.6 12.4 %reshape.221 = bf16[50,128,4,128]{3,2,1,0:T(4,128)(2,1)} reshape(bf16[50,128,512]{2,1,0:T(8,128)(2,1)} %param.21) | data formatting | bytes 13107200 | tf_op jit(solution)/shard_map/reshape | solution.py:131
  113.7 2.3 reshape.259
  121.6 6.8 %select_reduce_fusion.1 = (f32[50,4,4,4]{3,2,1,0:T(4,128)S(1)}, f32[50,4,4,4,128]{4,3,2,1,0:T(4,128)S(1)}) fusion(pred[50,4,128]{2,1,0:T(4,128)(4,1)S(1)} %or_and_fusion, bf16[50,4,4,4,128]{4,3,1,2,0:T(4,128)(2,1)} %gather_fusion.1, bf16[50,128,4,128,1]{3,2,1,0,4:T(4,128)(2,1)} %bitcast.71), kind=kOutput, calls=%fused_computation.28 | convolution fusion | flops 106083200 | bytes 9049600 | tf_op jit(solution)/shard_map/nsagh,nbah->nasgb/dot_general | solution.py:37
  129.5 49.1 %pmax.7 = f32[64,4,4,4]{0,3,2,1:T(4,128)S(1)} all-reduce(f32[64,4,4,4]{0,3,2,1:T(4,128)S(1)} %select_reduce_fusion), channel_id=1, replica_groups=mesh['row'=2,'col'=2,'seq'=8] {'seq'}, use_global_device_ids=true, to_apply=%region_5.6 | all-reduce | flops 4096 | bytes 32768 | tf_op jit(solution)/shard_map/pmax | solution.py:173
  178.7 2.8 fusion.23
  183.8 4.8 %fusion.20 = f32[50,4,4,4,128]{4,3,2,1,0:T(4,128)S(1)} fusion(bf16[50,128,4,128,1]{3,2,1,0,4:T(4,128)(2,1)} %bitcast.70, f32[50,4,4,4,128]{4,3,2,1,0:T(4,128)} %copy-done.5, f32[50,4,4,4]{3,2,1,0:T(4,128)S(1)} %bitcast.78, f32[50,4,4,4]{3,2,1,0:T(4,128)S(1)} %get-tuple-element.41, pred[50,4,128]{2,1,0:T(4,128)(4,1)S(1)} %copy-done.17), kind=kOutput, calls=%fused_computation.31 | convolution fusion | flops 106905600 | bytes 9881600 | tf_op jit(solution)/shard_map/nasgb,nbah->nasgh/dot_general | solution.py:54
  188.6 3.2 fusion.17
  196.5 9.3 %fusion.32 = f32[64,4,4,4,4]{3,4,2,1,0:T(4,128)S(1)} fusion(bf16[64,4,4,4,128]{4,3,2,0,1:T(4,128)(2,1)S(1)} %pad_maximum_fusion.1, bf16[64,4,4,64]{3,1,2,0:T(4,128)(2,1)S(1)} %get-tuple-element.31, bf16[64,4,4,64]{3,1,2,0:T(4,128)(2,1)S(1)} %get-tuple-element.30), kind=kOutput, calls=%fused_computation.49 | convolution fusion | flops 4718592 | bytes 1376256 | tf_op jit(solution)/shard_map/rsagh,ruah->rasgu/dot_general | solution.py:83
  210.0 33.9 %psum.15 = bf16[64,4,4,4]{0,3,2,1:T(4,128)(2,1)S(1)} all-reduce(bf16[64,4,4,4]{0,3,2,1:T(4,128)(2,1)S(1)} %convert_element_type.84), channel_id=1, replica_groups=mesh['row'=2,'col'=2,'seq'=8] {'seq'}, use_global_device_ids=true, to_apply=%region_9.10 | all-reduce | flops 4096 | bytes 16384 | tf_op jit(solution)/shard_map/psum | solution.py:179
  245.5 68.4 %all-gather.9.cloned.1.call-done = bf16[512,4,4,4,128]{4,0,3,2,1:T(8,128)(2,1)} async-done(((bf16[64,4,4,4,128]{4,0,3,2,1:T(8,128)(2,1)}), bf16[512,4,4,4,128]{4,0,3,2,1:T(8,128)(2,1)}) %all-gather.9.cloned.1.call-update) | async-done | bytes 8388624 | tf_op jit(solution)/shard_map/all_gather | solution.py:176
  313.9 5.7 %reduce_sum.40 = bf16[64,4,4,4,128]{4,0,3,2,1:T(8,128)(2,1)S(1)} reduce(bf16[8,64,4,4,4,128]{5,1,0,4,3,2:T(8,128)(2,1)} %bitcast.69, bf16[]{:T(256)} %constant.35.clone.1), dimensions={0}, to_apply=%region_6.7 | reduce | flops 3670016 | bytes 9437186 | tf_op jit(solution)/shard_map/reduce_sum | solution.py:175
  324.2 8.7 %all-gather.7.cloned.1.call-done = bf16[128,4,2048]{2,0,1:T(8,128)(2,1)} async-done(((bf16[64,4,2048]{2,0,1:T(8,128)(2,1)}), bf16[128,4,2048]{2,0,1:T(8,128)(2,1)}) %all-gather.7.cloned.1.call-update) | async-done | bytes 2097168 | tf_op jit(solution)/shard_map/all_gather | solution.py:192
  332.8 10.0 %fusion.6 = bf16[128,4,2560]{2,0,1:T(8,128)(2,1)} fusion(bf16[128,4,2048]{2,0,1:T(8,128)(2,1)} %all-gather.7.cloned.1.call-done, bf16[2048,2560]{1,0:T(8,128)(2,1)} %param.16), kind=kOutput, calls=%fused_computation.9 | convolution fusion | flops 5370019840 | bytes 15204352 | tf_op jit(solution)/shard_map/dot_general | solution.py:194
  345.0 36.8 %reduce-scatter.2.cloned.1.call-done = bf16[64,4,2560]{2,0,1:T(8,128)(2,1)} async-done(((bf16[128,4,2560]{2,0,1:T(8,128)(2,1)}), bf16[64,4,2560]{2,0,1:T(8,128)(2,1)}) %reduce-scatter.2.cloned.1.call-update) | async-done | bytes 1310736 | tf_op jit(solution)/shard_map/reduce_scatter | solution.py:198
  381.8 3.4 copy.167
  (110 shorter events, 37.5 us)
Async XLA Ops:
  7.2 55.3 %copy-start = (bf16[2560,512]{1,0:T(8,128)(2,1)S(1)}, bf16[2560,512]{1,0:T(8,128)(2,1)}, u32[]{:S(2)}) copy-start(bf16[2560,512]{1,0:T(8,128)(2,1)} %param.15) | copy-start | bytes 7864324
  7.2 50.0 %all-gather.5.cloned.1.call-start = ((), (), s32[]{:S(2)}) async-start(), calls=%async_computation.1 | async-start | bytes 3932160 | tf_op jit(solution)/shard_map/all_gather | solution.py:140
  15.4 93.3 %all-reduce.3.cloned.1.call-start = ((), (), s32[]{:S(2)}) async-start(), calls=%async_computation.5 | async-start | bytes 6291456
  62.4 3.4 copy-start.4
  62.4 3.4 copy-start.22
  78.9 234.9 %all-gather.9.cloned.1.call-start = ((), (), s32[]{:S(2)}) async-start(), calls=%async_computation.4 | async-start | bytes 9437184 | tf_op jit(solution)/shard_map/all_gather | solution.py:176
  94.6 12.4 %copy-start.24 = (u32[32]{0:T(128)S(1)}, u32[32]{0:T(128)}, u32[]{:S(2)}) copy-start(u32[32]{0:T(128)} %constant.42) | copy-start | bytes 388
  94.6 13.6 %copy-start.23 = (s32[50]{0:T(128)S(1)}, s32[50]{0:T(128)}, u32[]{:S(2)}) copy-start(s32[50]{0:T(128)} %param.19) | copy-start | bytes 604
  108.7 70.0 %copy-start.16 = (pred[50,4,128]{2,1,0:T(4,128)(4,1)}, pred[50,4,128]{2,1,0:T(4,128)(4,1)S(1)}, u32[]{:S(2)}) copy-start(pred[50,4,128]{2,1,0:T(4,128)(4,1)S(1)} %or_and_fusion) | copy-start | bytes 76804
  110.5 1.6 copy-start.3
  128.4 50.2 %copy-start.5 = (f32[50,4,4,4,128]{4,3,2,1,0:T(4,128)}, f32[50,4,4,4,128]{4,3,2,1,0:T(4,128)S(1)}, u32[]{:S(2)}) copy-start(f32[50,4,4,4,128]{4,3,2,1,0:T(4,128)S(1)} %get-tuple-element.42) | copy-start | bytes 4915204
  178.6 5.1 %copy-start.14 = (f32[64,4,4,4]{0,3,2,1:T(4,128)}, f32[64,4,4,4]{0,3,2,1:T(4,128)S(1)}, u32[]{:S(2)}) copy-start(f32[64,4,4,4]{0,3,2,1:T(4,128)S(1)} %pmax.7) | copy-start | bytes 49156
  181.5 2.3 copy-start.17
  183.7 4.8 %copy-start.19 = (s32[50]{0:T(128)S(1)}, s32[50]{0:T(128)}, u32[]{:S(2)}) copy-start(s32[50]{0:T(128)} %param.18) | copy-start | bytes 604
  188.5 6.7 %copy-start.7 = (f32[64,4,64]{2,1,0:T(4,128)S(1)}, f32[64,4,64]{2,1,0:T(4,128)}, u32[]{:S(2)}) copy-start(f32[64,4,64]{2,1,0:T(4,128)} %copy-done.6) | copy-start | bytes 196612
  188.5 6.7 %copy-start.9 = (f32[64,4,64]{2,1,0:T(4,128)S(1)}, f32[64,4,64]{2,1,0:T(4,128)}, u32[]{:S(2)}) copy-start(f32[64,4,64]{2,1,0:T(4,128)} %copy-done.8) | copy-start | bytes 196612
  191.8 141.1 %all-gather.7.cloned.1.call-start = ((), (), s32[]{:S(2)}) async-start(), calls=%async_computation.2 | async-start | bytes 3145728 | tf_op jit(solution)/shard_map/all_gather | solution.py:192
  205.8 1.3 copy-start.21
  205.8 3.9 copy-start.20
  205.8 38.0 %copy-start.15 = (f32[64,4,4,4]{0,3,2,1:T(4,128)S(1)}, f32[64,4,4,4]{0,3,2,1:T(4,128)}, u32[]{:S(2)}) copy-start(f32[64,4,4,4]{0,3,2,1:T(4,128)} %copy-done.14) | copy-start | bytes 49156
  323.9 57.9 %reduce-scatter.2.cloned.1.call-start = ((), (), s32[]{:S(2)}) async-start(), calls=%async_computation.3 | async-start | bytes 3932160 | tf_op jit(solution)/shard_map/reduce_scatter | solution.py:198
  342.9 0.9 copy-start.11
  342.9 1.0 copy-start.13
  343.9 41.3 %copy-start.1 = (bf16[2560,512]{1,0:T(8,128)(2,1)S(1)}, bf16[2560,512]{1,0:T(8,128)(2,1)}, u32[]{:S(2)}) copy-start(bf16[2560,512]{1,0:T(8,128)(2,1)} %param.15) | copy-start | bytes 7864324
  (6 other events, 4.2 us)
Sparse Core Ops, SparseCore 0:
  15.5 41.5 all-gather.4
  79.1 23.2 all-reduce.2
  191.9 121.9 all-gather.8
  324.0 8.7 all-gather.6
  343.0 38.7 reduce-scatter.1
